TPU v7x, 512 devices: a whole 4x8x8 slice. The times are simulated.
512 devices in a mesh: dp: 32 (over z, y_lo, core), feat: 16 (over y_hi, x).
Axes of the slice: x: 4, y: 8 (y_hi: 4, y_lo: 2; y = y_hi * 2 + y_lo), z: 8, core: 2. Of those that a mesh axis runs over, the one named last changes fastest.
Arguments:
- tokens: bfloat16 [8192, 8192], P('dp', 'feat'), may hold values from -6 to 6
- up_left: bfloat16 [16, 512, 2048], P('feat', 'dp'), may hold values from -0.25 to 0.25
- up_right: bfloat16 [2048, 16, 16], P('feat'), may hold values from -1.5 to 1.5
- down_left: bfloat16 [16, 2048, 512], P('feat', 'dp'), may hold values from -0.125 to 0.125
- down_right: bfloat16 [512, 16, 16], P('feat'), may hold values from -1.5 to 1.5
- layer_grad: bfloat16 [8192, 8192], P('dp', 'feat'), may hold values from -6 to 6
Outputs:
- layer_out: bfloat16 [8192, 8192], P('dp', 'feat')
- grad_tokens: bfloat16 [8192, 8192], P('dp', 'feat')
- grad_up_left: float32 [16, 512, 2048], P('feat', 'dp')
- grad_up_right: float32 [2048, 16, 16], P('feat')
- grad_down_left: float32 [16, 2048, 512], P('feat', 'dp')
- grad_down_right: float32 [512, 16, 16], P('feat')
All inputs are finite; a program needn't handle non-finite values.
Results may differ from a plain program's by a relative error of at most 0.0067.
Values may be sent and summed in bfloat16 or wider, within the bound.
No kernel may reach another device: no remote copies, remote signals or barrier semaphores. Data moves between devices by JAX's collectives and lax.ppermute only.
A program may use at most 128 MiB of HBM per device.

v0:
```python
import jax
import jax.numpy as jnp
import numpy as np
from jax import lax
from jax.sharding import Mesh
from jax.sharding import PartitionSpec as P

TILE_UP = 128
TILE_DOWN = 32
DP_AXES = ("z", "ylo", "core")
FEAT_AXES = ("yhi", "x")


def split_mesh(mesh):
    n_dp = mesh.shape["dp"]
    n_feat = mesh.shape["feat"]
    sizes = (n_dp // 4, 2, 2, n_feat // 4, 4)
    devices = np.asarray(mesh.devices).reshape(sizes)
    return Mesh(devices, DP_AXES + FEAT_AXES)


def exchange(wired):
    rows, feat_count, piece = wired.shape
    n_x = lax.axis_size("x")
    n_y = feat_count // n_x
    shaped = wired.reshape(rows, n_y, n_x, piece)
    shaped = lax.all_to_all(shaped, "x", 2, 2, tiled=True)
    shaped = lax.all_to_all(shaped, "yhi", 1, 1, tiled=True)
    return shaped.reshape(rows, feat_count, piece)


def dp_reduce_scatter(part, row_axis):
    shape = part.shape
    rows = shape[row_axis]
    n_z = lax.axis_size("z")
    split = shape[:row_axis] + (n_z, 2, 2, rows // (4 * n_z)) + shape[row_axis + 1 :]
    x = part.reshape(split)
    x = lax.psum_scatter(x, "core", scatter_dimension=row_axis + 2, tiled=True)
    x = lax.psum_scatter(x, "z", scatter_dimension=row_axis, tiled=True)
    x = lax.psum_scatter(x, "ylo", scatter_dimension=row_axis + 1, tiled=True)
    return x.reshape(shape[:row_axis] + (rows // (4 * n_z),) + shape[row_axis + 1 :])


def dp_all_gather(local, row_axis):
    shape = local.shape
    rows = shape[row_axis]
    x = local.reshape(shape[:row_axis] + (1, 1, 1, rows) + shape[row_axis + 1 :])
    x = lax.all_gather(x, "ylo", axis=row_axis + 1, tiled=True)
    x = lax.all_gather(x, "z", axis=row_axis, tiled=True)
    x = lax.all_gather(x, "core", axis=row_axis + 2, tiled=True)
    total = x.shape[row_axis] * x.shape[row_axis + 1] * x.shape[row_axis + 2] * rows
    return x.reshape(shape[:row_axis] + (total,) + shape[row_axis + 1 :])


def to_wire(blocks, feat_count):
    tok_rows, local_blocks, full_width = blocks.shape
    piece = full_width // feat_count
    shaped = blocks.reshape(tok_rows, local_blocks, feat_count, piece).transpose(0, 2, 1, 3)
    return shaped.reshape(tok_rows, feat_count, local_blocks * piece)


def from_wire(wired, local_blocks):
    tok_rows, feat_count, line_len = wired.shape
    piece = line_len // local_blocks
    shaped = wired.reshape(tok_rows, feat_count, local_blocks, piece).transpose(0, 2, 1, 3)
    return shaped.reshape(tok_rows, local_blocks, feat_count * piece)


def on_device(tokens, up_left, up_right, down_left, down_right, layer_grad):
    tok_rows = tokens.shape[0]
    local_blocks = up_left.shape[0]
    hidden_width = up_left.shape[2]
    block_width = down_left.shape[2]
    blocks_all = up_right.shape[1]
    group_up = up_right.shape[0]
    group_down = down_right.shape[0]
    feat_count = lax.axis_size("yhi") * lax.axis_size("x")
    n_dp = lax.axis_size("z") * lax.axis_size("ylo") * lax.axis_size("core")
    grad_scale = float(tok_rows * n_dp) ** (-0.5)
    tiles_up = group_up // TILE_UP
    tiles_down = group_down // TILE_DOWN
    up_full = dp_all_gather(up_left, 1)
    token_blocks = tokens.reshape(tok_rows, local_blocks, block_width)
    up_inner = jnp.einsum(
        "tbi,big->tbg", token_blocks, up_full, preferred_element_type=jnp.float32
    ).astype(jnp.bfloat16)
    up_mixed = exchange(to_wire(up_inner, feat_count))
    preact = jnp.einsum("tjg,gjk->tkg", up_mixed, up_right, preferred_element_type=jnp.float32)
    sigmoid_val = jax.nn.sigmoid(preact)
    activated = (
        (preact * sigmoid_val)
        .reshape(tok_rows, blocks_all, tiles_up, TILE_UP)
        .transpose(0, 2, 1, 3)
    )
    hidden = activated.reshape(tok_rows, local_blocks, hidden_width).astype(jnp.bfloat16)
    down_full = dp_all_gather(down_left, 1)
    down_inner = jnp.einsum(
        "tbh,bhc->tbc", hidden, down_full, preferred_element_type=jnp.float32
    ).astype(jnp.bfloat16)
    down_mixed = exchange(to_wire(down_inner, feat_count)).reshape(
        tok_rows, blocks_all * group_down
    )
    identity = jnp.eye(group_down, dtype=jnp.bfloat16).reshape(group_down, tiles_down, TILE_DOWN)
    mix_matrix = jnp.einsum(
        "cjk,cal->jcakl", down_right, identity, preferred_element_type=jnp.float32
    )
    mix_matrix = mix_matrix.astype(jnp.bfloat16).reshape(
        blocks_all * group_down, blocks_all * group_down
    )
    layer_out = jnp.dot(down_mixed, mix_matrix, preferred_element_type=jnp.float32).astype(
        jnp.bfloat16
    )
    grad_down_mixed = lax.dot_general(
        layer_grad, mix_matrix, (((1,), (1,)), ((), ())), preferred_element_type=jnp.float32
    ).astype(jnp.bfloat16)
    grad_by_group = layer_grad.reshape(tok_rows, tiles_down, blocks_all, TILE_DOWN).transpose(
        0, 2, 1, 3
    )
    grad_by_group = grad_by_group.reshape(tok_rows, blocks_all, group_down)
    right_down_term = (
        jnp.einsum(
            "tjc,tkc->cjk",
            down_mixed.reshape(tok_rows, blocks_all, group_down),
            grad_by_group,
            preferred_element_type=jnp.float32,
        )
        * grad_scale
    )
    grad_down_inner = from_wire(
        exchange(grad_down_mixed.reshape(tok_rows, feat_count, local_blocks * group_down)),
        local_blocks,
    )
    grad_down_left = dp_reduce_scatter(
        jnp.einsum("tbh,tbc->hbc", hidden, grad_down_inner, preferred_element_type=jnp.float32)
        * grad_scale,
        0,
    ).transpose(1, 0, 2)
    grad_hidden = jnp.einsum(
        "tbc,bhc->tbh", grad_down_inner, down_full, preferred_element_type=jnp.float32
    )
    grad_hidden = grad_hidden.reshape(tok_rows, tiles_up, blocks_all, TILE_UP).transpose(0, 2, 1, 3)
    grad_hidden = grad_hidden.reshape(tok_rows, blocks_all, group_up)
    grad_preact = (grad_hidden * sigmoid_val * (1.0 + preact * (1.0 - sigmoid_val))).astype(
        jnp.bfloat16
    )
    grad_up_mixed = jnp.einsum(
        "tkg,gjk->tjg", grad_preact, up_right, preferred_element_type=jnp.float32
    ).astype(jnp.bfloat16)
    right_up_term = (
        jnp.einsum("tjg,tkg->gjk", up_mixed, grad_preact, preferred_element_type=jnp.float32)
        * grad_scale
    )
    grad_up_inner = from_wire(exchange(grad_up_mixed), local_blocks)
    grad_tokens = jnp.einsum(
        "tbg,big->tbi", grad_up_inner, up_full, preferred_element_type=jnp.float32
    ).astype(jnp.bfloat16)
    grad_tokens = grad_tokens.reshape(tok_rows, local_blocks * block_width)
    grad_up_left = dp_reduce_scatter(
        jnp.einsum("tbi,tbg->ibg", token_blocks, grad_up_inner, preferred_element_type=jnp.float32)
        * grad_scale,
        0,
    ).transpose(1, 0, 2)
    rights = jnp.concatenate([right_up_term, right_down_term], axis=0)
    rights = lax.psum(rights, DP_AXES)
    grad_up_right = rights[:group_up]
    grad_down_right = rights[group_up:]
    return (layer_out, grad_tokens, grad_up_left, grad_up_right, grad_down_left, grad_down_right)


def solution(mesh):
    fine = split_mesh(mesh)
    row = P(DP_AXES, FEAT_AXES)
    weight = P(FEAT_AXES, DP_AXES, None)
    mixer = P(FEAT_AXES, None, None)
    return jax.shard_map(
        on_device,
        mesh=fine,
        in_specs=(row, weight, mixer, weight, mixer, row),
        out_specs=(row, row, weight, mixer, weight, mixer),
        check_vma=False,
    )
```

profile of v0, /device:TPU:1, one launch (start us, length us, event | category | flops | bytes accessed | tf_op | source)
XLA Modules:
  0.0 650.3 jit_solution(2913419054008153790)
XLA Ops:
  7.2 6.3 all-gather
  13.6 42.4 %all-gather.13.cloned.1.call-done = bf16[16,16,2048]{2,1,0:T(8,128)(2,1)} async-done(((bf16[2,16,2048]{2,1,0:T(8,128)(2,1)}), bf16[16,16,2048]{2,1,0:T(8,128)(2,1)}) %all-gather.13.cloned.1.call-update) | async-done | bytes 1048592 | tf_op jit(solution)/shard_map/all_gather | solution.py:49
  56.1 5.3 all-gather.2
  66.9 4.0 all-to-all-start.4
  70.8 10.1 %all-gather.9.cloned.1.call-done = bf16[1,8,2,2,16,2048]{5,4,3,2,1,0:T(8,128)(2,1)} async-done(((bf16[1,8,2,1,16,2048]{5,4,3,2,1,0:T(8,128)(2,1)}), bf16[1,8,2,2,16,2048]{5,4,3,2,1,0:T(8,128)(2,1)}) %all-gather.9.cloned.1.call-update) | async-done | bytes 2097168 | tf_op jit(solution)/shard_map/all_gather | solution.py:50
  80.9 2.3 convolution_convert_fusion
  84.4 3.5 all-to-all-start
  87.9 32.6 %all-gather.15.cloned.1.call-done = bf16[16,64,512]{2,1,0:T(8,128)(2,1)} async-done(((bf16[2,64,512]{2,1,0:T(8,128)(2,1)}), bf16[16,64,512]{2,1,0:T(8,128)(2,1)}) %all-gather.15.cloned.1.call-update) | async-done | bytes 1048592 | tf_op jit(solution)/shard_map/all_gather | solution.py:49
  121.3 6.5 all-to-all-start.5
  128.8 6.9 %all-to-all-done.5 = bf16[256,4,4,32]{0,3,2,1:T(8,128)(2,1)S(1)} async-done(((bf16[256,4,4,32]{0,3,2,1:T(8,128)(2,1)}), bf16[256,4,4,32]{0,3,2,1:T(8,128)(2,1)S(1)}, u32[]{:S(2)}, u32[]{:S(2)}) %all-to-all-start.5) | async-done | bytes 262176 | tf_op jit(solution)/shard_map/all_to_all | solution.py:28
  135.7 4.3 all-to-all-start.1
  141.2 4.1 all-gather.11.cloned.1.call-done
  147.6 18.1 %all-to-all-done.1 = bf16[256,4,4,128]{0,3,2,1:T(8,128)(2,1)} async-done(((bf16[256,4,4,128]{0,3,2,1:T(8,128)(2,1)}), bf16[256,4,4,128]{0,3,2,1:T(8,128)(2,1)}, u32[]{:S(2)}, u32[]{:S(2)}) %all-to-all-start.1) | async-done | bytes 1048608 | tf_op jit(solution)/shard_map/all_to_all | solution.py:28
  165.8 4.5 fusion.7
  172.3 15.0 %all_to_all.40 = bf16[256,4,4,128]{0,3,1,2:T(8,128)(2,1)S(1)} all-to-all(bf16[256,4,4,128]{0,3,1,2:T(8,128)(2,1)S(1)} %copy.95), channel_id=1, replica_groups=mesh['z'=8,'ylo'=2,'core'=2,'yhi'=4,'x'=4] {'x'}, dimensions={2} | all-to-all | bytes 2097152 | tf_op jit(solution)/shard_map/all_to_all | solution.py:27
  188.4 6.5 %all-to-all-start.7 = ((bf16[256,4,4,128]{0,3,2,1:T(8,128)(2,1)}), bf16[256,4,4,128]{0,3,2,1:T(8,128)(2,1)S(1)}, u32[]{:S(2)}, u32[]{:S(2)}) async-start(bf16[256,4,4,128]{0,3,2,1:T(8,128)(2,1)} %copy.96), calls=%async_computation.7 | async-start | bytes 2097152 | tf_op jit(solution)/shard_map/all_to_all | solution.py:28
  196.3 2.7 multiply_bitcast_fusion
  199.0 5.4 copy.103
  204.5 10.2 %all-to-all-done.7 = bf16[256,4,4,128]{0,3,2,1:T(8,128)(2,1)S(1)} async-done(((bf16[256,4,4,128]{0,3,2,1:T(8,128)(2,1)}), bf16[256,4,4,128]{0,3,2,1:T(8,128)(2,1)S(1)}, u32[]{:S(2)}, u32[]{:S(2)}) %all-to-all-start.7) | async-done | bytes 1048608 | tf_op jit(solution)/shard_map/all_to_all | solution.py:28
  214.7 2.7 convolution_multiply_fusion
  218.7 53.0 %all-reduce.8.cloned.1.call-done = (f32[8,2,2,16,1,2048]{5,3,4,2,1,0:T(8,128)}, f32[8,2,2,64,1,512]{5,3,2,1,0,4:T(8,128)}) async-done(((f32[8,2,2,16,1,2048]{5,3,4,2,1,0:T(8,128)}, f32[8,2,2,64,1,512]{5,3,2,1,0,4:T(8,128)}), (f32[8,2,2,16,1,2048]{5,3,4,2,1,0:T(8,128)}, f32[8,2,2,64,1,512]{5,3,2,1,0,4:T(8,128)})) %all-reduce.8.cloned.1.call-update) | async-done | bytes 8388624
  271.7 3.9 constant_dynamic-slice_fusion
  275.6 3.9 constant_dynamic-slice_fusion.1
  283.2 9.2 %all_to_all.41 = bf16[256,4,4,32]{0,3,1,2:T(8,128)(2,1)S(1)} all-to-all(bf16[256,4,4,32]{0,3,1,2:T(8,128)(2,1)S(1)} %copy.87), channel_id=1, replica_groups=mesh['z'=8,'ylo'=2,'core'=2,'yhi'=4,'x'=4] {'x'}, dimensions={2} | all-to-all | bytes 524288 | tf_op jit(solution)/shard_map/all_to_all | solution.py:27
  293.1 6.5 all-to-all-start.3
  302.9 5.1 all-to-all-done.3
  309.3 7.6 %reduce-scatter.13.cloned.1.call-done = f32[1,2,1,64,1,512]{5,3,2,1,0,4:T(8,128)} async-done(((f32[8,2,1,64,1,512]{5,3,2,1,0,4:T(8,128)}), f32[1,2,1,64,1,512]{5,3,2,1,0,4:T(8,128)}) %reduce-scatter.13.cloned.1.call-update) | async-done | bytes 262160 | tf_op jit(solution)/shard_map/reduce_scatter | solution.py:39
  317.0 46.2 %reduce-scatter.9.cloned.1.call-done = f32[1,2,1,16,1,2048]{5,3,4,2,1,0:T(8,128)} async-done(((f32[8,2,1,16,1,2048]{5,3,4,2,1,0:T(8,128)}), f32[1,2,1,16,1,2048]{5,3,4,2,1,0:T(8,128)}) %reduce-scatter.9.cloned.1.call-update) | async-done | bytes 262160 | tf_op jit(solution)/shard_map/reduce_scatter | solution.py:39
  364.3 233.1 %all-reduce.6.cloned.1.call-done = f32[160,16,16]{0,2,1:T(8,128)} async-done(((f32[160,16,16]{0,2,1:T(8,128)}), f32[160,16,16]{0,2,1:T(8,128)}) %all-reduce.6.cloned.1.call-update) | async-done | bytes 163856 | tf_op jit(solution)/shard_map/psum | solution.py:164
  600.6 3.0 convolution_convert_fusion.2
  603.6 16.7 %reduce-scatter.15.cloned.1.call-done = f32[1,1,1,64,1,512]{5,3,2,1,0,4:T(8,128)} async-done(((f32[1,2,1,64,1,512]{5,3,2,1,0,4:T(8,128)}), f32[1,1,1,64,1,512]{5,3,2,1,0,4:T(8,128)}) %reduce-scatter.15.cloned.1.call-update) | async-done | bytes 131088 | tf_op jit(solution)/shard_map/reduce_scatter | solution.py:40
  620.3 23.2 %reduce-scatter.11.cloned.1.call-done = f32[1,1,1,16,1,2048]{5,3,4,2,1,0:T(8,128)} async-done(((f32[1,2,1,16,1,2048]{5,3,4,2,1,0:T(8,128)}), f32[1,1,1,16,1,2048]{5,3,4,2,1,0:T(8,128)}) %reduce-scatter.11.cloned.1.call-update) | async-done | bytes 131088 | tf_op jit(solution)/shard_map/reduce_scatter | solution.py:40
  (76 shorter events, 31.2 us)
Async XLA Ops:
  7.2 73.8 %copy-start = (bf16[256,512]{1,0:T(8,128)(2,1)S(1)}, bf16[256,512]{1,0:T(8,128)(2,1)}, u32[]{:S(2)}) copy-start(bf16[256,512]{1,0:T(8,128)(2,1)} %param.6) | copy-start | bytes 786436
  7.2 48.8 %all-gather.13.cloned.1.call-start = ((), (), s32[]{:S(2)}) async-start(), calls=%async_computation.19 | async-start | bytes 1179648 | tf_op jit(solution)/shard_map/all_gather | solution.py:49
  13.6 67.3 %all-gather.9.cloned.1.call-start = ((), (), s32[]{:S(2)}) async-start(), calls=%async_computation.12 | async-start | bytes 3145728 | tf_op jit(solution)/shard_map/all_gather | solution.py:50
  56.0 64.5 %all-gather.15.cloned.1.call-start = ((), (), s32[]{:S(2)}) async-start(), calls=%async_computation.20 | async-start | bytes 1179648 | tf_op jit(solution)/shard_map/all_gather | solution.py:49
  62.3 3.5 copy-start.9
  66.9 17.5 %all-to-all-start.4 = ((bf16[256,4,4,32]{0,3,1,2:T(8,128)(2,1)}), bf16[256,4,4,32]{0,3,1,2:T(8,128)(2,1)S(1)}, u32[]{:S(2)}, u32[]{:S(2)}) async-start(bf16[256,4,4,32]{0,3,1,2:T(8,128)(2,1)} %copy.90), calls=%async_computation.4 | async-start | bytes 524288 | tf_op jit(solution)/shard_map/all_to_all | solution.py:27
  84.4 37.0 %all-to-all-start = ((bf16[256,4,4,128]{0,3,1,2:T(8,128)(2,1)}), bf16[256,4,4,128]{0,3,1,2:T(8,128)(2,1)S(1)}, u32[]{:S(2)}, u32[]{:S(2)}) async-start(bf16[256,4,4,128]{0,3,1,2:T(8,128)(2,1)} %copy.81), calls=%async_computation | async-start | bytes 2097152 | tf_op jit(solution)/shard_map/all_to_all | solution.py:27
  87.9 57.4 %all-gather.11.cloned.1.call-start = ((), (), s32[]{:S(2)}) async-start(), calls=%async_computation.13 | async-start | bytes 3145728 | tf_op jit(solution)/shard_map/all_gather | solution.py:50
  121.3 14.4 %all-to-all-start.5 = ((bf16[256,4,4,32]{0,3,2,1:T(8,128)(2,1)}), bf16[256,4,4,32]{0,3,2,1:T(8,128)(2,1)S(1)}, u32[]{:S(2)}, u32[]{:S(2)}) async-start(bf16[256,4,4,32]{0,3,2,1:T(8,128)(2,1)} %copy.91), calls=%async_computation.5 | async-start | bytes 524288 | tf_op jit(solution)/shard_map/all_to_all | solution.py:28
  127.8 12.2 %copy-start.11 = (bf16[128,16,16]{0,2,1:T(8,128)(2,1)S(1)}, bf16[128,16,16]{0,2,1:T(8,128)(2,1)}, u32[]{:S(2)}) copy-start(bf16[128,16,16]{0,2,1:T(8,128)(2,1)} %param.8) | copy-start | bytes 196612
  135.7 30.0 %all-to-all-start.1 = ((bf16[256,4,4,128]{0,3,2,1:T(8,128)(2,1)}), bf16[256,4,4,128]{0,3,2,1:T(8,128)(2,1)}, u32[]{:S(2)}, u32[]{:S(2)}) async-start(bf16[256,4,4,128]{0,3,2,1:T(8,128)(2,1)} %copy.82), calls=%async_computation.1 | async-start | bytes 2097152 | tf_op jit(solution)/shard_map/all_to_all | solution.py:28
  165.7 5.5 copy-start.7
  170.2 1.0 copy-start.2
  187.3 7.6 %copy-start.8 = (bf16[256,16,128]{0,1,2:T(8,128)(2,1)S(1)}, bf16[256,16,128]{0,1,2:T(8,128)(2,1)}, u32[]{:S(2)}) copy-start(bf16[256,16,128]{0,1,2:T(8,128)(2,1)} %get-tuple-element.21) | copy-start | bytes 3145732
  188.4 26.3 %all-to-all-start.7 = ((bf16[256,4,4,128]{0,3,2,1:T(8,128)(2,1)}), bf16[256,4,4,128]{0,3,2,1:T(8,128)(2,1)S(1)}, u32[]{:S(2)}, u32[]{:S(2)}) async-start(bf16[256,4,4,128]{0,3,2,1:T(8,128)(2,1)} %copy.96), calls=%async_computation.7 | async-start | bytes 2097152 | tf_op jit(solution)/shard_map/all_to_all | solution.py:28
  194.9 76.8 %all-reduce.8.cloned.1.call-start = ((), (), s32[]{:S(2)}) async-start(), calls=%async_computation.21 | async-start | bytes 16777216
  195.2 1.1 copy-start.6
  214.7 2.7 copy-start.4
  217.4 99.6 %reduce-scatter.13.cloned.1.call-start = ((), (), s32[]{:S(2)}) async-start(), calls=%async_computation.17 | async-start | bytes 2359296 | tf_op jit(solution)/shard_map/reduce_scatter | solution.py:39
  275.6 87.7 %reduce-scatter.9.cloned.1.call-start = ((), (), s32[]{:S(2)}) async-start(), calls=%async_computation.14 | async-start | bytes 2359296 | tf_op jit(solution)/shard_map/reduce_scatter | solution.py:39
  279.5 1.6 copy-start.1
  283.1 17.4 %copy-start.3 = (bf16[256,16,128]{0,1,2:T(8,128)(2,1)S(1)}, bf16[256,16,128]{0,1,2:T(8,128)(2,1)}, u32[]{:S(2)}) copy-start(bf16[256,16,128]{0,1,2:T(8,128)(2,1)} %copy-done.2) | copy-start | bytes 3145732
  293.1 14.8 %all-to-all-start.3 = ((bf16[256,4,4,32]{0,3,2,1:T(8,128)(2,1)}), bf16[256,4,4,32]{0,3,2,1:T(8,128)(2,1)S(1)}, u32[]{:S(2)}, u32[]{:S(2)}) async-start(bf16[256,4,4,32]{0,3,2,1:T(8,128)(2,1)} %copy.88), calls=%async_computation.3 | async-start | bytes 524288 | tf_op jit(solution)/shard_map/all_to_all | solution.py:28
  299.6 297.9 %all-reduce.6.cloned.1.call-start = ((), (), s32[]{:S(2)}) async-start(), calls=%async_computation.16 | async-start | bytes 524288 | tf_op jit(solution)/shard_map/psum | solution.py:164
  300.4 7.5 %copy-start.10 = (bf16[256,512]{0,1:T(8,128)(2,1)S(1)}, bf16[256,512]{0,1:T(8,128)(2,1)}, u32[]{:S(2)}) copy-start(bf16[256,512]{0,1:T(8,128)(2,1)} %copy.99) | copy-start | bytes 786436
  302.9 297.7 %copy-start.5 = (bf16[256,4,4,128]{0,3,2,1:T(8,128)(2,1)S(1)}, bf16[256,4,4,128]{0,3,2,1:T(8,128)(2,1)}, u32[]{:S(2)}) copy-start(bf16[256,4,4,128]{0,3,2,1:T(8,128)(2,1)} %copy-done.4) | copy-start | bytes 3145732
  309.3 311.0 %reduce-scatter.15.cloned.1.call-start = ((), (), s32[]{:S(2)}) async-start(), calls=%async_computation.18 | async-start | bytes 393216 | tf_op jit(solution)/shard_map/reduce_scatter | solution.py:40
  317.0 326.5 %reduce-scatter.11.cloned.1.call-start = ((), (), s32[]{:S(2)}) async-start(), calls=%async_computation.15 | async-start | bytes 393216 | tf_op jit(solution)/shard_map/reduce_scatter | solution.py:40
Sparse Core Ops, SparseCore 0:
  13.7 42.2 all-gather.12
  58.1 22.8 all-gather.8
  83.0 37.5 all-gather.14
  122.5 22.7 all-gather.10
  217.5 54.1 all-reduce.7
  275.7 41.1 reduce-scatter.12
  319.8 43.4 reduce-scatter.8
  366.7 230.6 all-reduce.5
  601.0 19.2 reduce-scatter.14
  623.5 19.9 reduce-scatter.10
where the time goes:
time: 652 us; the launch traced here: 650 us
  waiting for transfers between devices  509 us (78%)
  blocking collectives  35.8 us (5%)
  local copies, waits for them, and re-layouts  33.3 us (5%)
  starting transfers between devices  31.5 us (5%)
  matrix products  23.7 us (4%)
  between operations  14.3 us (2%)
    psum x1, waiting for transfers between devices, on_device(): rights = lax.psum(rights, DP_AXES)  233 us
    all_gather x2, waiting for transfers between devices, dp_all_gather(): x = lax.all_gather(x, 'z', axis=row_axis, tiled=True)  75 us
    reduce_scatter x2, waiting for transfers between devices, dp_reduce_scatter(): x = lax.psum_scatter(x, 'z', scatter_dimension=row_axis, tiled=True)  53.9 us
    unnamed x11, waiting for transfers between devices  53.1 us
    all_to_all x4, waiting for transfers between devices, exchange(): shaped = lax.all_to_all(shaped, 'yhi', 1, 1, tiled=True)  40.3 us
    reduce_scatter x2, waiting for transfers between devices, dp_reduce_scatter(): x = lax.psum_scatter(x, 'ylo', scatter_dimension=row_axis + 1, tiled=True)  39.8 us
    all_to_all x2, blocking collectives, exchange(): shaped = lax.all_to_all(shaped, 'x', 2, 2, tiled=True)  24.2 us
    all_to_all x4, starting transfers between devices, exchange(): shaped = lax.all_to_all(shaped, 'yhi', 1, 1, tiled=True)  23.7 us
  transfers between devices with their start and end apart: 16, of which 14 were waited for; matrix products, arithmetic and copies ran while one was open for 7% of the time, Pallas kernels for 0%

commit v1 on v0

--- a/solution.py
+++ b/solution.py
@@ -24,7 +24,9 @@
     n_x = lax.axis_size("x")
     n_y = feat_count // n_x
     shaped = wired.reshape(rows, n_y, n_x, piece)
-    shaped = lax.all_to_all(shaped, "x", 2, 2, tiled=True)
+    shaped = jnp.concatenate(
+        lax.all_to_all(jnp.stack(jnp.split(shaped, lax.axis_size("x"), axis=2)), "x", 0, 0), axis=2
+    )
     shaped = lax.all_to_all(shaped, "yhi", 1, 1, tiled=True)
     return shaped.reshape(rows, feat_count, piece)
 

time: 652 us -> 658 us (level)
    unnamed x29 -> x33, local copies, waits for them, and re-layouts: 14.7 us -> 18.2 us
  transfers between devices with their start and end apart: 16 -> 16, of which waited for: 14 -> 14; matrix products, arithmetic and copies ran while one was open for 7% -> 6% of each run, Pallas kernels for 0% -> 0%
where the time goes in v1:
time: 658 us; the launch traced here: 657 us
  waiting for transfers between devices  509 us (77%)
  local copies, waits for them, and re-layouts  37.6 us (6%)
  blocking collectives  35.8 us (5%)
  starting transfers between devices  31.5 us (5%)
  matrix products  23.7 us (4%)
  between operations  14.4 us (2%)
    psum x1, waiting for transfers between devices, on_device(): rights = lax.psum(rights, DP_AXES)  233 us
    all_gather x2, waiting for transfers between devices, dp_all_gather(): x = lax.all_gather(x, 'z', axis=row_axis, tiled=True)  74.9 us
    reduce_scatter x2, waiting for transfers between devices, dp_reduce_scatter(): x = lax.psum_scatter(x, 'z', scatter_dimension=row_axis, tiled=True)  53.9 us
    unnamed x11, waiting for transfers between devices  53.2 us
    all_to_all x4, waiting for transfers between devices, exchange(): shaped = lax.all_to_all(shaped, 'yhi', 1, 1, tiled=True)  40.3 us
    reduce_scatter x2, waiting for transfers between devices, dp_reduce_scatter(): x = lax.psum_scatter(x, 'ylo', scatter_dimension=row_axis + 1, tiled=True)  39.8 us
    all_to_all x2, blocking collectives, exchange(): lax.all_to_all(jnp.stack(jnp.split(shaped, lax.axis_size('x'), axis=2)),...  24.2 us
    all_to_all x4, starting transfers between devices, exchange(): shaped = lax.all_to_all(shaped, 'yhi', 1, 1, tiled=True)  23.7 us
  transfers between devices with their start and end apart: 16, of which 14 were waited for; matrix products, arithmetic and copies ran while one was open for 6% of the time, Pallas kernels for 0%

profile of v1, /device:TPU:1, one launch (start us, length us, event | category | flops | bytes accessed | tf_op | source)
XLA Modules:
  0.0 656.6 jit_solution(9736136021768040966)
XLA Ops:
  7.2 6.3 all-gather
  13.6 42.4 %all-gather.13.cloned.1.call-done = bf16[16,16,2048]{2,1,0:T(8,128)(2,1)} async-done(((bf16[2,16,2048]{2,1,0:T(8,128)(2,1)}), bf16[16,16,2048]{2,1,0:T(8,128)(2,1)}) %all-gather.13.cloned.1.call-update) | async-done | bytes 1048592 | tf_op jit(solution)/shard_map/all_gather | solution.py:51
  56.1 5.3 all-gather.2
  66.9 4.0 all-to-all-start.4
  70.9 10.1 %all-gather.9.cloned.1.call-done = bf16[1,8,2,2,16,2048]{5,4,3,2,1,0:T(8,128)(2,1)} async-done(((bf16[1,8,2,1,16,2048]{5,4,3,2,1,0:T(8,128)(2,1)}), bf16[1,8,2,2,16,2048]{5,4,3,2,1,0:T(8,128)(2,1)}) %all-gather.9.cloned.1.call-update) | async-done | bytes 2097168 | tf_op jit(solution)/shard_map/all_gather | solution.py:52
  80.9 2.4 convolution_convert_fusion
  84.5 3.5 all-to-all-start
  88.1 32.5 %all-gather.15.cloned.1.call-done = bf16[16,64,512]{2,1,0:T(8,128)(2,1)} async-done(((bf16[2,64,512]{2,1,0:T(8,128)(2,1)}), bf16[16,64,512]{2,1,0:T(8,128)(2,1)}) %all-gather.15.cloned.1.call-update) | async-done | bytes 1048592 | tf_op jit(solution)/shard_map/all_gather | solution.py:51
  121.3 6.5 all-to-all-start.5
  128.8 6.9 %all-to-all-done.5 = bf16[256,4,4,32]{0,3,2,1:T(8,128)(2,1)S(1)} async-done(((bf16[256,4,4,32]{0,3,2,1:T(8,128)(2,1)}), bf16[256,4,4,32]{0,3,2,1:T(8,128)(2,1)S(1)}, u32[]{:S(2)}, u32[]{:S(2)}) %all-to-all-start.5) | async-done | bytes 262176 | tf_op jit(solution)/shard_map/all_to_all | solution.py:30
  135.7 4.3 all-to-all-start.1
  141.2 4.1 all-gather.11.cloned.1.call-done
  147.6 18.1 %all-to-all-done.1 = bf16[256,4,4,128]{0,3,2,1:T(8,128)(2,1)} async-done(((bf16[256,4,4,128]{0,3,2,1:T(8,128)(2,1)}), bf16[256,4,4,128]{0,3,2,1:T(8,128)(2,1)}, u32[]{:S(2)}, u32[]{:S(2)}) %all-to-all-start.1) | async-done | bytes 1048608 | tf_op jit(solution)/shard_map/all_to_all | solution.py:30
  165.7 4.5 fusion.7
  177.9 15.0 %all_to_all.40 = bf16[4,256,4,1,128]{4,1,3,2,0:T(8,128)(2,1)S(1)} all-to-all(bf16[4,256,4,1,128]{4,1,3,2,0:T(8,128)(2,1)S(1)} %pad_maximum_fusion.1), channel_id=1, replica_groups=mesh['z'=8,'ylo'=2,'core'=2,'yhi'=4,'x'=4] {'x'}, dimensions={0} | all-to-all | bytes 2097152 | tf_op jit(solution)/shard_map/all_to_all | solution.py:28
  194.0 6.5 all-to-all-start.7
  201.9 2.7 multiply_bitcast_fusion
  204.7 5.4 copy.133
  210.1 10.2 %all-to-all-done.7 = bf16[256,4,4,128]{3,0,2,1:T(8,128)(2,1)S(1)} async-done(((bf16[256,4,4,128]{3,0,2,1:T(8,128)(2,1)}), bf16[256,4,4,128]{3,0,2,1:T(8,128)(2,1)S(1)}, u32[]{:S(2)}, u32[]{:S(2)}) %all-to-all-start.7) | async-done | bytes 1048608 | tf_op jit(solution)/shard_map/all_to_all | solution.py:30
  220.9 2.7 convolution_multiply_fusion
  224.9 53.0 %all-reduce.8.cloned.1.call-done = (f32[8,2,2,16,1,2048]{5,3,4,2,1,0:T(8,128)}, f32[8,2,2,64,1,512]{5,3,2,1,0,4:T(8,128)}) async-done(((f32[8,2,2,16,1,2048]{5,3,4,2,1,0:T(8,128)}, f32[8,2,2,64,1,512]{5,3,2,1,0,4:T(8,128)}), (f32[8,2,2,16,1,2048]{5,3,4,2,1,0:T(8,128)}, f32[8,2,2,64,1,512]{5,3,2,1,0,4:T(8,128)})) %all-reduce.8.cloned.1.call-update) | async-done | bytes 8388624
  278.0 3.9 constant_dynamic-slice_fusion
  281.9 3.9 constant_dynamic-slice_fusion.1
  289.6 9.2 %all_to_all.41 = bf16[4,256,4,1,32]{1,4,2,3,0:T(8,128)(2,1)S(1)} all-to-all(bf16[4,256,4,1,32]{1,4,2,3,0:T(8,128)(2,1)S(1)} %pad_maximum_fusion.2), channel_id=1, replica_groups=mesh['z'=8,'ylo'=2,'core'=2,'yhi'=4,'x'=4] {'x'}, dimensions={0} | all-to-all | bytes 524288 | tf_op jit(solution)/shard_map/all_to_all | solution.py:28
  299.5 6.4 all-to-all-start.3
  309.2 5.1 all-to-all-done.3
  315.6 7.6 %reduce-scatter.13.cloned.1.call-done = f32[1,2,1,64,1,512]{5,3,2,1,0,4:T(8,128)} async-done(((f32[8,2,1,64,1,512]{5,3,2,1,0,4:T(8,128)}), f32[1,2,1,64,1,512]{5,3,2,1,0,4:T(8,128)}) %reduce-scatter.13.cloned.1.call-update) | async-done | bytes 262160 | tf_op jit(solution)/shard_map/reduce_scatter | solution.py:41
  323.3 46.3 %reduce-scatter.9.cloned.1.call-done = f32[1,2,1,16,1,2048]{5,3,4,2,1,0:T(8,128)} async-done(((f32[8,2,1,16,1,2048]{5,3,4,2,1,0:T(8,128)}), f32[1,2,1,16,1,2048]{5,3,4,2,1,0:T(8,128)}) %reduce-scatter.9.cloned.1.call-update) | async-done | bytes 262160 | tf_op jit(solution)/shard_map/reduce_scatter | solution.py:41
  370.6 233.1 %all-reduce.6.cloned.1.call-done = f32[160,16,16]{0,2,1:T(8,128)} async-done(((f32[160,16,16]{0,2,1:T(8,128)}), f32[160,16,16]{0,2,1:T(8,128)}) %all-reduce.6.cloned.1.call-update) | async-done | bytes 163856 | tf_op jit(solution)/shard_map/psum | solution.py:166
  606.9 3.0 convolution_convert_fusion.2
  609.9 16.7 %reduce-scatter.15.cloned.1.call-done = f32[1,1,1,64,1,512]{5,3,2,1,0,4:T(8,128)} async-done(((f32[1,2,1,64,1,512]{5,3,2,1,0,4:T(8,128)}), f32[1,1,1,64,1,512]{5,3,2,1,0,4:T(8,128)}) %reduce-scatter.15.cloned.1.call-update) | async-done | bytes 131088 | tf_op jit(solution)/shard_map/reduce_scatter | solution.py:42
  626.6 23.2 %reduce-scatter.11.cloned.1.call-done = f32[1,1,1,16,1,2048]{5,3,4,2,1,0:T(8,128)} async-done(((f32[1,2,1,16,1,2048]{5,3,4,2,1,0:T(8,128)}), f32[1,1,1,16,1,2048]{5,3,4,2,1,0:T(8,128)}) %reduce-scatter.11.cloned.1.call-update) | async-done | bytes 131088 | tf_op jit(solution)/shard_map/reduce_scatter | solution.py:42
  (85 shorter events, 37.5 us)
Async XLA Ops:
  7.2 73.8 %copy-start = (bf16[256,512]{1,0:T(8,128)(2,1)S(1)}, bf16[256,512]{1,0:T(8,128)(2,1)}, u32[]{:S(2)}) copy-start(bf16[256,512]{1,0:T(8,128)(2,1)} %param.6) | copy-start | bytes 786436
  7.2 48.8 %all-gather.13.cloned.1.call-start = ((), (), s32[]{:S(2)}) async-start(), calls=%async_computation.19 | async-start | bytes 1179648 | tf_op jit(solution)/shard_map/all_gather | solution.py:51
  13.6 67.3 %all-gather.9.cloned.1.call-start = ((), (), s32[]{:S(2)}) async-start(), calls=%async_computation.12 | async-start | bytes 3145728 | tf_op jit(solution)/shard_map/all_gather | solution.py:52
  56.0 64.5 %all-gather.15.cloned.1.call-start = ((), (), s32[]{:S(2)}) async-start(), calls=%async_computation.20 | async-start | bytes 1179648 | tf_op jit(solution)/shard_map/all_gather | solution.py:51
  62.3 3.5 copy-start.9
  66.9 17.6 %all-to-all-start.4 = ((bf16[4,256,4,1,32]{1,4,2,3,0:T(8,128)(2,1)}), bf16[4,256,4,1,32]{1,4,2,3,0:T(8,128)(2,1)S(1)}, u32[]{:S(2)}, u32[]{:S(2)}) async-start(bf16[4,256,4,1,32]{1,4,2,3,0:T(8,128)(2,1)} %pad_maximum_fusion.3), calls=%async_computation.4 | async-start | bytes 524288 | tf_op jit(solution)/shard_map/all_to_all | solution.py:28
  84.5 36.8 %all-to-all-start = ((bf16[4,256,4,1,128]{1,4,2,3,0:T(8,128)(2,1)}), bf16[4,256,4,1,128]{1,4,2,3,0:T(8,128)(2,1)S(1)}, u32[]{:S(2)}, u32[]{:S(2)}) async-start(bf16[4,256,4,1,128]{1,4,2,3,0:T(8,128)(2,1)} %pad_maximum_fusion), calls=%async_computation | async-start | bytes 2097152 | tf_op jit(solution)/shard_map/all_to_all | solution.py:28
  88.0 57.3 %all-gather.11.cloned.1.call-start = ((), (), s32[]{:S(2)}) async-start(), calls=%async_computation.13 | async-start | bytes 3145728 | tf_op jit(solution)/shard_map/all_gather | solution.py:52
  121.3 14.4 %all-to-all-start.5 = ((bf16[256,4,4,32]{0,3,2,1:T(8,128)(2,1)}), bf16[256,4,4,32]{0,3,2,1:T(8,128)(2,1)S(1)}, u32[]{:S(2)}, u32[]{:S(2)}) async-start(bf16[256,4,4,32]{0,3,2,1:T(8,128)(2,1)} %bitcast.178), calls=%async_computation.5 | async-start | bytes 524288 | tf_op jit(solution)/shard_map/all_to_all | solution.py:30
  127.8 12.2 %copy-start.11 = (bf16[128,16,16]{0,2,1:T(8,128)(2,1)S(1)}, bf16[128,16,16]{0,2,1:T(8,128)(2,1)}, u32[]{:S(2)}) copy-start(bf16[128,16,16]{0,2,1:T(8,128)(2,1)} %param.8) | copy-start | bytes 196612
  135.7 30.0 %all-to-all-start.1 = ((bf16[256,4,4,128]{0,3,2,1:T(8,128)(2,1)}), bf16[256,4,4,128]{0,3,2,1:T(8,128)(2,1)}, u32[]{:S(2)}, u32[]{:S(2)}) async-start(bf16[256,4,4,128]{0,3,2,1:T(8,128)(2,1)} %copy.103), calls=%async_computation.1 | async-start | bytes 2097152 | tf_op jit(solution)/shard_map/all_to_all | solution.py:30
  165.7 5.5 copy-start.7
  170.2 1.0 copy-start.2
  193.0 7.6 %copy-start.8 = (bf16[256,16,128]{0,1,2:T(8,128)(2,1)S(1)}, bf16[256,16,128]{0,1,2:T(8,128)(2,1)}, u32[]{:S(2)}) copy-start(bf16[256,16,128]{0,1,2:T(8,128)(2,1)} %get-tuple-element.21) | copy-start | bytes 3145732
  194.0 26.3 %all-to-all-start.7 = ((bf16[256,4,4,128]{3,0,2,1:T(8,128)(2,1)}), bf16[256,4,4,128]{3,0,2,1:T(8,128)(2,1)S(1)}, u32[]{:S(2)}, u32[]{:S(2)}) async-start(bf16[256,4,4,128]{3,0,2,1:T(8,128)(2,1)} %copy.125), calls=%async_computation.7 | async-start | bytes 2097152 | tf_op jit(solution)/shard_map/all_to_all | solution.py:30
  200.5 77.4 %all-reduce.8.cloned.1.call-start = ((), (), s32[]{:S(2)}) async-start(), calls=%async_computation.21 | async-start | bytes 16777216
  200.9 1.1 copy-start.6
  220.9 2.7 copy-start.4
  223.6 99.6 %reduce-scatter.13.cloned.1.call-start = ((), (), s32[]{:S(2)}) async-start(), calls=%async_computation.17 | async-start | bytes 2359296 | tf_op jit(solution)/shard_map/reduce_scatter | solution.py:41
  281.9 87.7 %reduce-scatter.9.cloned.1.call-start = ((), (), s32[]{:S(2)}) async-start(), calls=%async_computation.14 | async-start | bytes 2359296 | tf_op jit(solution)/shard_map/reduce_scatter | solution.py:41
  285.8 1.6 copy-start.1
  289.3 17.4 %copy-start.3 = (bf16[256,16,128]{0,1,2:T(8,128)(2,1)S(1)}, bf16[256,16,128]{0,1,2:T(8,128)(2,1)}, u32[]{:S(2)}) copy-start(bf16[256,16,128]{0,1,2:T(8,128)(2,1)} %copy-done.2) | copy-start | bytes 3145732
  299.5 14.8 %all-to-all-start.3 = ((bf16[256,4,4,32]{0,3,2,1:T(8,128)(2,1)}), bf16[256,4,4,32]{0,3,2,1:T(8,128)(2,1)S(1)}, u32[]{:S(2)}, u32[]{:S(2)}) async-start(bf16[256,4,4,32]{0,3,2,1:T(8,128)(2,1)} %copy.111), calls=%async_computation.3 | async-start | bytes 524288 | tf_op jit(solution)/shard_map/all_to_all | solution.py:30
  305.9 297.8 %all-reduce.6.cloned.1.call-start = ((), (), s32[]{:S(2)}) async-start(), calls=%async_computation.16 | async-start | bytes 524288 | tf_op jit(solution)/shard_map/psum | solution.py:166
  306.8 7.5 %copy-start.10 = (bf16[256,512]{0,1:T(8,128)(2,1)S(1)}, bf16[256,512]{0,1:T(8,128)(2,1)}, u32[]{:S(2)}) copy-start(bf16[256,512]{0,1:T(8,128)(2,1)} %copy.129) | copy-start | bytes 786436
  309.2 297.6 %copy-start.5 = (bf16[256,4,4,128]{0,3,2,1:T(8,128)(2,1)S(1)}, bf16[256,4,4,128]{0,3,2,1:T(8,128)(2,1)}, u32[]{:S(2)}) copy-start(bf16[256,4,4,128]{0,3,2,1:T(8,128)(2,1)} %copy-done.4) | copy-start | bytes 3145732
  315.6 311.0 %reduce-scatter.15.cloned.1.call-start = ((), (), s32[]{:S(2)}) async-start(), calls=%async_computation.18 | async-start | bytes 393216 | tf_op jit(solution)/shard_map/reduce_scatter | solution.py:42
  323.3 326.5 %reduce-scatter.11.cloned.1.call-start = ((), (), s32[]{:S(2)}) async-start(), calls=%async_computation.15 | async-start | bytes 393216 | tf_op jit(solution)/shard_map/reduce_scatter | solution.py:42
Sparse Core Ops, SparseCore 0:
  13.7 42.2 all-gather.12
  58.1 22.8 all-gather.8
  83.0 37.5 all-gather.14
  122.5 22.7 all-gather.10
  223.7 54.2 all-reduce.7
  282.0 41.2 reduce-scatter.12
  326.1 43.4 reduce-scatter.8
  373.1 230.6 all-reduce.5
  607.3 19.2 reduce-scatter.14
  629.8 19.9 reduce-scatter.10
